TPU v7x, 256 devices: a whole 4x4x8 slice. The times are simulated.
256 devices in a mesh: batch: 8 (over x, core), tensor: 32 (over y, z).
Axes of the slice: x: 4, y: 4, z: 8, core: 2. Of those that a mesh axis runs over, the one named last changes fastest.
Arguments:
- inputs: bfloat16 [4, 8, 32, 4096], P(None, 'batch', 'tensor'), may hold values from -6 to 6
- norm_gain: float32 [4096], replicated, may hold values from 0.5 to 1.5
- norm_bias: float32 [4096], replicated, may hold values from -3 to 3
- qkv_weight: bfloat16 [4096, 3, 4096], P(None, None, 'tensor'), may hold values from -0.09375 to 0.09375
- out_weight: bfloat16 [4096, 4096], P('tensor'), may hold values from -0.375 to 0.375
- in_weight: bfloat16 [4096, 8192], P(None, 'tensor'), may hold values from -0.09375 to 0.09375
- in_bias: float32 [8192], P('tensor'), may hold values from -3 to 3
- down_weight: bfloat16 [8192, 4096], P('tensor'), may hold values from -0.0625 to 0.0625
- down_bias: float32 [4096], replicated, may hold values from -3 to 3
- page_pool: bfloat16 [128, 2, 128, 4096], P('batch', None, None, 'tensor'), may hold values from -103 to 103
- old_cache: bfloat16 [8, 32, 2, 64, 4096], P('batch', None, None, None, 'tensor'), may hold values from -103 to 103, as said below
- page_table: int32 [32, 4], replicated, may hold values from 0 to 127, as said below
- prompt_length: int32 [32], replicated, may hold values from 1 to 512, 8192 in all
- parents: int32 [4, 8, 32], replicated, may hold values from 0 to 7
Outputs:
- outputs: float32 [4, 8, 32, 4096], P(None, 'batch', 'tensor')
Inputs may be any that keep to these rules, and one draw needn't show every extreme that they name: `old_cache`: key and value entries of the beams' generated tokens. `page_table`: every pool page is named exactly once in the table. The pool is cut into as many equal blocks of consecutive pages as the batch axis has devices; request r names only pages of block r modulo that count.
All inputs are finite; a program needn't handle non-finite values.
Results may differ from a plain program's by a relative error of at most 0.034.
Values may be sent and summed in bfloat16 or wider, within the bound.
No kernel may reach another device: no remote copies, remote signals or barrier semaphores. Data moves between devices by JAX's collectives and lax.ppermute only.
A program may use at most 128 MiB of HBM per device.

v0:
```python
import math
import jax
import jax.numpy as jnp
from jax import lax
from jax.sharding import PartitionSpec as P

HDIM = 256
ROT = 64
BEAMS = 8
NEG_FILL = -1e30


def partner(value, axis, bit):
    return lax.ppermute(value, axis, [(i, i ^ 1 << bit) for i in range(lax.axis_size(axis))])


def normalize(row_block, norm_gain, norm_bias):
    widened = row_block.astype(jnp.float32)
    center = jnp.mean(widened, axis=-1, keepdims=True)
    shifted = widened - center
    variance = jnp.mean(shifted * shifted, axis=-1, keepdims=True)
    return shifted * lax.rsqrt(variance + 1e-05) * norm_gain + norm_bias


def rotate_local(vectors, position, first_column):
    half_count = vectors.shape[-1] // 2
    doubled = (first_column + 2 * jnp.arange(half_count)) % HDIM
    exponent = doubled.astype(jnp.float32) / ROT
    frequency = jnp.where(doubled < ROT, jnp.exp(-exponent * math.log(10000.0)), 0.0)
    angles = position[..., None] * frequency
    cosine = jnp.cos(angles)
    sine_part = jnp.sin(angles)
    halves = vectors.reshape(vectors.shape[:-1] + (half_count, 2))
    even_part = halves[..., 0]
    odd_part = halves[..., 1]
    turned = jnp.stack(
        [even_part * cosine - odd_part * sine_part, odd_part * cosine + even_part * sine_part],
        axis=-1,
    )
    return turned.reshape(vectors.shape)


def on_device(
    inputs,
    norm_gain,
    norm_bias,
    qkv_weight,
    out_weight,
    in_weight,
    in_bias,
    down_weight,
    down_bias,
    page_pool,
    old_cache,
    page_table,
    prompt_length,
    parents,
):
    batch_index = lax.axis_index("batch")
    tensor_index = lax.axis_index("tensor")
    groups = lax.axis_size("batch")
    steps = inputs.shape[0]
    model_width = inputs.shape[3]
    columns = qkv_weight.shape[2]
    requests = page_table.shape[0]
    history = old_cache.shape[3]
    page_count = page_table.shape[1]
    page_size = page_pool.shape[2]
    pool_dev = page_pool.shape[0]
    prompt_span = page_count * page_size
    local_reqs = requests // groups
    scale_factor = HDIM ** (-0.5)
    first_column = tensor_index * columns
    normed = normalize(inputs[:, 0], norm_gain, norm_bias).astype(jnp.bfloat16)
    rows = lax.all_gather(normed, "tensor", axis=1, tiled=True)
    flat = rows.reshape(steps * requests, model_width)
    qkv_flat = qkv_weight.reshape(model_width, 3 * columns)
    projected = jnp.dot(flat, qkv_flat, preferred_element_type=jnp.float32).reshape(
        steps, requests, 3 * columns
    )
    ffn = jnp.dot(flat, in_weight, preferred_element_type=jnp.float32).reshape(steps, requests, -1)
    hidden = jax.nn.gelu(ffn + in_bias, approximate=True).astype(jnp.bfloat16)
    position = (
        prompt_length[None, :] + history + jnp.arange(steps, dtype=jnp.int32)[:, None]
    ).astype(jnp.float32)
    queries = rotate_local(projected[..., :columns], position, first_column).astype(jnp.bfloat16)
    fresh_keys = rotate_local(projected[..., columns : 2 * columns], position, first_column).astype(
        jnp.bfloat16
    )
    fresh_values = projected[..., 2 * columns :].astype(jnp.bfloat16)
    query_all = lax.all_gather(queries[:, None], "batch", axis=1, tiled=True)
    beam_ids = jnp.broadcast_to(jnp.arange(BEAMS, dtype=jnp.int32)[:, None], (BEAMS, requests))
    new_ok_steps = []
    old_ok_steps = []
    for step_index in range(steps):
        lineage = beam_ids
        per_t = [None] * steps
        for back_step in range(step_index, -1, -1):
            per_t[back_step] = lineage == batch_index
            lineage = jnp.take_along_axis(parents[back_step], lineage, axis=0)
        for t in range(step_index + 1, steps):
            per_t[t] = jnp.zeros((BEAMS, requests), bool)
        new_ok_steps.append(jnp.stack(per_t, axis=-1))
        old_ok_steps.append(lineage == batch_index)
    new_ok = jnp.stack(new_ok_steps, axis=0)
    old_ok = jnp.stack(old_ok_steps, axis=0)
    old_keys = old_cache[0, :, 0]
    old_values = old_cache[0, :, 1]
    old_scores = jnp.einsum(
        "sbrc,rhc->sbrh", query_all, old_keys, preferred_element_type=jnp.float32
    )
    new_scores = jnp.einsum(
        "sbrc,trc->sbrt", query_all, fresh_keys, preferred_element_type=jnp.float32
    )
    query_local = lax.dynamic_index_in_dim(
        query_all.reshape(steps, BEAMS, local_reqs, groups, columns), batch_index, 3, False
    )
    table_local = (
        lax.dynamic_index_in_dim(
            page_table.reshape(local_reqs, groups, page_count), batch_index, 1, False
        )
        - batch_index * pool_dev
    )
    table_local = jnp.clip(table_local, 0, pool_dev - 1)
    length_local = lax.dynamic_index_in_dim(
        prompt_length.reshape(local_reqs, groups), batch_index, 1, False
    )
    pages = page_pool[table_local]
    prompt_keys = pages[:, :, 0].reshape(local_reqs, prompt_span, columns)
    prompt_values = pages[:, :, 1].reshape(local_reqs, prompt_span, columns)
    prompt_scores = jnp.einsum(
        "sbrc,rtc->sbrt", query_local, prompt_keys, preferred_element_type=jnp.float32
    )
    other = partner((old_scores, new_scores, prompt_scores), "tensor", 0)
    old_scores = (old_scores + other[0]) * scale_factor
    new_scores = (new_scores + other[1]) * scale_factor
    prompt_scores = (prompt_scores + other[2]) * scale_factor
    old_mask = old_ok[..., None]
    old_masked = jnp.where(old_mask, old_scores, NEG_FILL)
    new_masked = jnp.where(new_ok, new_scores, NEG_FILL)
    chain_peak = jnp.maximum(jnp.max(old_masked, axis=-1), jnp.max(new_masked, axis=-1))
    old_w = jnp.where(old_mask, jnp.exp(old_masked - chain_peak[..., None]), 0.0)
    new_w = jnp.where(new_ok, jnp.exp(new_masked - chain_peak[..., None]), 0.0)
    chain_total = jnp.sum(old_w, axis=-1) + jnp.sum(new_w, axis=-1)
    chain_mix = jnp.einsum(
        "sbrh,rhc->sbrc", old_w.astype(jnp.bfloat16), old_values, preferred_element_type=jnp.float32
    ) + jnp.einsum(
        "sbrt,trc->sbrc",
        new_w.astype(jnp.bfloat16),
        fresh_values,
        preferred_element_type=jnp.float32,
    )
    prompt_mask = (jnp.arange(prompt_span)[None, :] < length_local[:, None])[None, None]
    prompt_masked = jnp.where(prompt_mask, prompt_scores, NEG_FILL)
    prompt_peak = jnp.max(prompt_masked, axis=-1)
    prompt_w = jnp.where(prompt_mask, jnp.exp(prompt_masked - prompt_peak[..., None]), 0.0)
    prompt_total = jnp.sum(prompt_w, axis=-1)
    prompt_mix = jnp.einsum(
        "sbrt,rtc->sbrc",
        prompt_w.astype(jnp.bfloat16),
        prompt_values,
        preferred_element_type=jnp.float32,
    )
    slot_hit = (jnp.arange(groups) == batch_index)[None, None, None, :]

    def spread(values, fill):
        placed = jnp.where(slot_hit, values[..., None], fill)
        return placed.reshape(values.shape[:2] + (requests,))

    def spread_mix(values):
        placed = jnp.where(slot_hit[..., None], values[:, :, :, None, :], 0.0)
        return placed.reshape(values.shape[:2] + (requests, columns))

    p_peak = spread(prompt_peak, NEG_FILL)
    p_total = spread(prompt_total, 0.0)
    p_mix = spread_mix(prompt_mix)
    peak = jnp.maximum(chain_peak, p_peak)
    f_chain = jnp.exp(chain_peak - peak)
    f_prompt = jnp.exp(p_peak - peak)
    total = chain_total * f_chain + p_total * f_prompt
    mix = chain_mix * f_chain[..., None] + p_mix * f_prompt[..., None]
    packed = jnp.concatenate([mix, peak[..., None], total[..., None]], axis=-1)
    received = lax.all_to_all(packed, "batch", 1, 1, tiled=True)
    r_mix = received[..., :columns]
    r_peak = received[..., columns]
    r_total = received[..., columns + 1]
    g_peak = jnp.max(r_peak, axis=1, keepdims=True)
    factor = jnp.exp(r_peak - g_peak)
    all_total = jnp.sum(r_total * factor, axis=1)
    all_mix = jnp.sum(r_mix * factor[..., None], axis=1)
    attention = (all_mix / all_total[..., None]).astype(jnp.bfloat16)
    update = jnp.einsum(
        "src,cd->rsd", attention, out_weight, preferred_element_type=jnp.float32
    ) + jnp.einsum("srf,fd->rsd", hidden, down_weight, preferred_element_type=jnp.float32)
    summed = lax.psum_scatter(update, "tensor", scatter_dimension=0, tiled=True)
    result = inputs[:, 0].astype(jnp.float32) + jnp.transpose(summed, (1, 0, 2)) + down_bias
    return result[:, None]


def solution(mesh):
    in_specs = (
        P(None, "batch", "tensor", None),
        P(),
        P(),
        P(None, None, "tensor"),
        P("tensor", None),
        P(None, "tensor"),
        P("tensor"),
        P("tensor", None),
        P(),
        P("batch", None, None, "tensor"),
        P("batch", None, None, None, "tensor"),
        P(),
        P(),
        P(),
    )
    out_specs = P(None, "batch", "tensor", None)
    return jax.shard_map(
        on_device, mesh=mesh, in_specs=in_specs, out_specs=out_specs, check_vma=False
    )
```

profile of v0, /device:TPU:2, one launch (start us, length us, event | category | flops | bytes accessed | tf_op | source)
XLA Modules:
  0.0 358.6 jit_solution(18365220035608578066)
XLA Ops:
  8.6 1.5 fusion.85
  21.9 1.4 gather_fusion.5
  27.2 4.7 %copy.447 = bf16[4096,3,128]{0,2,1:T(8,128)(2,1)} copy(bf16[4096,3,128]{2,0,1:T(8,128)(2,1)} %param.19) | data formatting | bytes 6291456 | tf_op args[3]
  32.9 2.0 gather_fusion
  36.0 53.7 %all-gather.2.cloned.1.call-done = bf16[4,32,4096]{2,0,1:T(4,128)(2,1)} async-done(((bf16[4,1,4096]{2,0,1:T(4,128)(2,1)}), bf16[4,32,4096]{2,0,1:T(4,128)(2,1)}) %all-gather.2.cloned.1.call-update) | async-done | bytes 1048592 | tf_op jit(solution)/shard_map/all_gather | solution.py:75
  89.7 3.4 fusion.13
  95.4 12.8 %all_gather.7 = bf16[4,8,32,128]{3,2,0,1:T(8,128)(2,1)S(1)} all-gather(bf16[4,1,32,128]{3,2,0,1:T(8,128)(2,1)S(1)} %copy.454), channel_id=1, replica_groups=mesh['batch'=8,'tensor'=32] {'batch'}, dimensions={1}, use_global_device_ids=true | all-gather | bytes 294912 | tf_op jit(solution)/shard_map/all_gather | solution.py:91
  111.8 1.5 collective-permute-start
  115.5 3.4 collective-permute-done.1
  119.9 10.2 %collective-permute-done = f32[4,8,32,64]{3,1,0,2:T(8,128)S(1)} collective-permute-done((f32[4,8,32,64]{3,1,0,2:T(8,128)S(1)}, f32[4,8,32,64]{3,1,0,2:T(8,128)S(1)}, u32[]{:S(2)}, u32[]{:S(2)}) %collective-permute-start) | collective-permute-done | bytes 262176 | tf_op jit(solution)/shard_map/ppermute | solution.py:14
  130.6 4.6 %collective-permute-done.2 = f32[4,8,4,512]{3,1,0,2:T(8,128)S(1)} collective-permute-done((f32[4,8,4,512]{3,1,0,2:T(8,128)S(1)}, f32[4,8,4,512]{3,1,0,2:T(8,128)S(1)}, u32[]{:S(2)}, u32[]{:S(2)}) %collective-permute-start.2) | collective-permute-done | bytes 262176 | tf_op jit(solution)/shard_map/ppermute | solution.py:14
  139.5 1.6 fusion.21
  141.7 1.5 copy.478
  146.8 1.5 broadcast_in_dim.190
  149.8 1.5 broadcast_in_dim.187
  152.7 2.0 copy.481
  154.7 2.0 copy.482
  159.1 1.7 convolution_bitcast_fusion.1
  162.6 18.9 %all_to_all.5 = f32[4,8,32,130]{3,0,2,1:T(4,128)S(1)} all-to-all(f32[4,8,32,130]{3,0,2,1:T(4,128)S(1)} %copy.483), channel_id=1, replica_groups=mesh['batch'=8,'tensor'=32] {'batch'}, dimensions={1} | all-to-all | bytes 1064960 | tf_op jit(solution)/shard_map/all_to_all | solution.py:183
  186.4 3.0 fusion.10
  189.4 5.0 %fusion = f32[32,4,4096]{2,0,1:T(8,128)} fusion(f32[4,32,4096]{2,1,0:T(8,128)} %fusion.10, bf16[256,4096]{1,0:T(8,128)(2,1)S(1)} %copy-done, bf16[4096,256]{1,0:T(8,128)(2,1)} %param.21, bf16[4,32,4096]{2,0,1:T(4,128)(2,1)S(1)} %copy-done.1, f32[256]{0:T(256)S(1)} %copy-done.13), kind=kOutput, calls=%fused_computation.12 | convolution fusion | flops 537722880 | bytes 9438208 | tf_op jit(solution)/shard_map/srf,fd->rsd/dot_general | solution.py:194
  194.4 4.3 %copy.491 = f32[32,4,4096]{2,1,0:T(4,128)} copy(f32[32,4,4096]{2,0,1:T(8,128)} %fusion) | data formatting | bytes 4194304 | tf_op jit(solution)/shard_map/add | solution.py:192
  199.9 149.7 %all-reduce.3.cloned.1.call-done = f32[32,4,4096]{2,1,0:T(4,128)} async-done(((f32[32,4,4096]{2,1,0:T(4,128)}), f32[32,4,4096]{2,1,0:T(4,128)}) %all-reduce.3.cloned.1.call-update) | async-done | bytes 2097168
  349.6 1.5 fusion.86
  (155 shorter events, 51.3 us)
Async XLA Ops:
  6.5 182.9 %copy-start = (bf16[256,4096]{1,0:T(8,128)(2,1)S(1)}, bf16[256,4096]{1,0:T(8,128)(2,1)}, u32[]{:S(2)}) copy-start(bf16[256,4096]{1,0:T(8,128)(2,1)} %param.23) | copy-start | bytes 6291460
  6.5 83.1 %all-gather.2.cloned.1.call-start = ((), (), s32[]{:S(2)}) async-start(), calls=%async_computation.1 | async-start | bytes 1081344 | tf_op jit(solution)/shard_map/all_gather | solution.py:75
  10.1 339.5 %all-reduce.3.cloned.1.call-start = ((), (), s32[]{:S(2)}) async-start(), calls=%async_computation.2 | async-start | bytes 4194304
  27.2 4.9 %copy-start.12 = (s32[32,4]{0,1:T(4,128)S(1)}, s32[32,4]{0,1:T(4,128)}, u32[]{:S(2)}) copy-start(s32[32,4]{0,1:T(4,128)} %param.27) | copy-start | bytes 1540
  27.2 5.2 %copy-start.14 = (s32[32]{0:T(128)S(1)}, s32[32]{0:T(128)}, u32[]{:S(2)}) copy-start(s32[32]{0:T(128)} %param.28) | copy-start | bytes 388
  32.1 98.1 %copy-start.8 = (pred[4,8,32]{1,0,2:T(4,128)(4,1)}, pred[4,8,32]{1,0,2:T(4,128)(4,1)S(1)}, u32[]{:S(2)}) copy-start(pred[4,8,32]{1,0,2:T(4,128)(4,1)S(1)} %copy.446) | copy-start | bytes 3076
  109.7 9.2 %collective-permute-start.1 = (f32[4,8,32,4]{1,3,0,2:T(4,128)S(1)}, f32[4,8,32,4]{1,3,0,2:T(4,128)S(1)}, u32[]{:S(2)}, u32[]{:S(2)}) collective-permute-start(f32[4,8,32,4]{1,3,0,2:T(4,128)S(1)} %convolution_bitcast_fusion.4), channel_id=1, source_target_pairs={{0,1},{1,0},{2,3},{3,2},{4,5},{5,4},{6,7},{7,6},{8,9},{9,8},{10,11... | collective-permute-start | bytes 49160 | tf_op jit(solution)/shard_map/ppermute | solution.py:14
  111.8 18.4 %collective-permute-start = (f32[4,8,32,64]{3,1,0,2:T(8,128)S(1)}, f32[4,8,32,64]{3,1,0,2:T(8,128)S(1)}, u32[]{:S(2)}, u32[]{:S(2)}) collective-permute-start(f32[4,8,32,64]{3,1,0,2:T(8,128)S(1)} %convolution_bitcast_fusion.2), channel_id=1, source_target_pairs={{0,1},{1,0},{2,3},{3,2},{4,5},{5,4},{6,7},{7,6},{8,9},{9,8},{10,11... | collective-permute-start | bytes 786440 | tf_op jit(solution)/shard_map/ppermute | solution.py:14
  114.7 20.5 %collective-permute-start.2 = (f32[4,8,4,512]{3,1,0,2:T(8,128)S(1)}, f32[4,8,4,512]{3,1,0,2:T(8,128)S(1)}, u32[]{:S(2)}, u32[]{:S(2)}) collective-permute-start(f32[4,8,4,512]{3,1,0,2:T(8,128)S(1)} %convolution_bitcast_fusion.3), channel_id=1, source_target_pairs={{0,1},{1,0},{2,3},{3,2},{4,5},{5,4},{6,7},{7,6},{8,9},{9,8},{10,11... | collective-permute-start | bytes 786440 | tf_op jit(solution)/shard_map/ppermute | solution.py:14
  118.9 0.7 copy-start.5
  130.2 5.0 %copy-start.4 = (f32[4,8,32,64]{3,1,0,2:T(8,128)}, f32[4,8,32,64]{3,1,0,2:T(8,128)S(1)}, u32[]{:S(2)}) copy-start(f32[4,8,32,64]{3,1,0,2:T(8,128)S(1)} %collective-permute-done) | copy-start | bytes 786436
  159.0 1.8 copy-start.6
  159.0 1.8 copy-start.9
  159.1 1.8 copy-start.10
  160.8 1.0 copy-start.2
  160.8 1.2 copy-start.3
  185.6 3.8 %copy-start.13 = (f32[256]{0:T(256)S(1)}, f32[256]{0:T(256)}, u32[]{:S(2)}) copy-start(f32[256]{0:T(256)} %param.22) | copy-start | bytes 3076
  186.2 3.2 copy-start.1
  198.7 0.7 copy-start.15
  198.7 150.9 %copy-start.7 = (bf16[4,1,1,4096]{3,0,2,1:T(4,128)(2,1)S(1)}, bf16[4,1,1,4096]{3,0,2,1:T(4,128)(2,1)}, u32[]{:S(2)}) copy-start(bf16[4,1,1,4096]{3,0,2,1:T(4,128)(2,1)} %param.16) | copy-start | bytes 98308
  198.7 150.9 %copy-start.11 = (f32[4096]{0:T(1024)S(1)}, f32[4096]{0:T(1024)}, u32[]{:S(2)}) copy-start(f32[4096]{0:T(1024)} %param.24) | copy-start | bytes 49156
Sparse Core Ops, SparseCore 0:
  10.2 79.4 all-gather.1
  198.8 150.7 all-reduce.2
where the time goes:
time: 360 us; the launch traced here: 359 us
  waiting for transfers between devices  222 us (62%)
  local copies, waits for them, and re-layouts  52.6 us (15%)
  blocking collectives  31.7 us (9%)
  matrix products  18.8 us (5%)
  other arithmetic  17 us (5%)
  between operations  13.9 us (4%)
    unnamed x3, waiting for transfers between devices  150 us
    all_gather x1, waiting for transfers between devices, on_device(): rows = lax.all_gather(normed, 'tensor', axis=1, tiled=True)  53.7 us
    all_to_all x1, blocking collectives, on_device(): received = lax.all_to_all(packed, 'batch', 1, 1, tiled=True)  18.9 us
    ppermute x3, waiting for transfers between devices, partner(): lax.ppermute(value, axis, [(i, i ^ 1 << bit) for i in range(lax.axis_size...  18.2 us
    gather x27, local copies, waits for them, and re-layouts, on_device(): lineage = jnp.take_along_axis(parents[back_step], lineage, axis=0)  15.6 us
    all_gather x1, blocking collectives, on_device(): query_all = lax.all_gather(queries[:, None], 'batch', axis=1, tiled=True)  12.8 us
    unnamed x42, local copies, waits for them, and re-layouts  10.5 us
  transfers between devices with their start and end apart: 5, of which 5 were waited for; matrix products, arithmetic and copies ran while one was open for 8% of the time, Pallas kernels for 0%

commit v1 on v0

--- a/solution.py
+++ b/solution.py
@@ -72,7 +72,10 @@
     scale_factor = HDIM ** (-0.5)
     first_column = tensor_index * columns
     normed = normalize(inputs[:, 0], norm_gain, norm_bias).astype(jnp.bfloat16)
-    rows = lax.all_gather(normed, "tensor", axis=1, tiled=True)
+    size = lax.axis_size("tensor")
+    blocks = jnp.stack([normed for _ in range(size)])
+    blocks = lax.all_to_all(blocks, "tensor", split_axis=0, concat_axis=0)
+    rows = jnp.concatenate(blocks, axis=1)
     flat = rows.reshape(steps * requests, model_width)
     qkv_flat = qkv_weight.reshape(model_width, 3 * columns)
     projected = jnp.dot(flat, qkv_flat, preferred_element_type=jnp.float32).reshape(

time: 360 us -> 341 us (0.947)
  waiting for transfers between devices: 222 us -> 172 us
  local copies, waits for them, and re-layouts: 52.6 us -> 66.6 us
  starting transfers between devices: 3.01 us -> 15.8 us
  other arithmetic: 17 us -> 21.2 us
    all_gather x1 -> x0, waiting for transfers between devices: 53.7 us -> none  [on_device(): rows = lax.all_gather(normed, 'tensor', axis=1, tiled=True)]
    all_to_all x0 -> x1, starting transfers between devices: none -> 11.5 us  [on_device(): blocks = lax.all_to_all(blocks, 'tensor', split_axis=0, concat_axis=0)]
    unnamed x42 -> x62, local copies, waits for them, and re-layouts: 10.5 us -> 16.1 us
    unnamed x3 -> x2, waiting for transfers between devices: 150 us -> 154 us
  transfers between devices with their start and end apart: 5 -> 5, of which waited for: 5 -> 4; matrix products, arithmetic and copies ran while one was open for 8% -> 10% of each run, Pallas kernels for 0% -> 0%
where the time goes in v1:
time: 341 us; the launch traced here: 339 us
  waiting for transfers between devices  172 us (50%)
  local copies, waits for them, and re-layouts  66.6 us (20%)
  blocking collectives  32 us (9%)
  other arithmetic  21.2 us (6%)
  matrix products  17.7 us (5%)
  starting transfers between devices  15.8 us (5%)
  between operations  13.9 us (4%)
    unnamed x2, waiting for transfers between devices  154 us
    all_to_all x1, blocking collectives, on_device(): received = lax.all_to_all(packed, 'batch', 1, 1, tiled=True)  18.9 us
    ppermute x3, waiting for transfers between devices, partner(): lax.ppermute(value, axis, [(i, i ^ 1 << bit) for i in range(lax.axis_size...  18.4 us
    unnamed x62, local copies, waits for them, and re-layouts  16.1 us
    gather x27, local copies, waits for them, and re-layouts, on_device(): lineage = jnp.take_along_axis(parents[back_step], lineage, axis=0)  15.6 us
    all_gather x1, blocking collectives, on_device(): query_all = lax.all_gather(queries[:, None], 'batch', axis=1, tiled=True)  13.1 us
    all_to_all x1, starting transfers between devices, on_device(): blocks = lax.all_to_all(blocks, 'tensor', split_axis=0, concat_axis=0)  11.5 us
  transfers between devices with their start and end apart: 5, of which 4 were waited for; matrix products, arithmetic and copies ran while one was open for 10% of the time, Pallas kernels for 0%

profile of v1, /device:TPU:2, one launch (start us, length us, event | category | flops | bytes accessed | tf_op | source)
XLA Modules:
  0.0 339.1 jit_solution(14016843338539248133)
XLA Ops:
  10.9 11.5 %all-to-all-start = ((bf16[32,4,1,4096]{3,1,2,0:T(4,128)(2,1)}), bf16[32,4,1,4096]{3,1,2,0:T(4,128)(2,1)S(1)}, u32[]{:S(2)}, u32[]{:S(2)}) async-start(bf16[32,4,1,4096]{3,1,2,0:T(4,128)(2,1)} %stack.55), calls=%async_computation | async-start | bytes 2097152 | tf_op jit(solution)/shard_map/all_to_all | solution.py:77
  38.9 4.7 %copy.446 = bf16[4096,3,128]{0,2,1:T(8,128)(2,1)} copy(bf16[4096,3,128]{2,0,1:T(8,128)(2,1)} %param.19) | data formatting | bytes 6291456 | tf_op args[3]
  45.0 2.9 gather_fusion
  49.8 2.3 fusion.129
  52.1 3.0 fusion.11
  58.4 1.6 copy.504
  65.9 13.1 %all_gather.3 = bf16[4,8,32,128]{3,2,0,1:T(8,128)(2,1)S(1)} all-gather(bf16[4,1,32,128]{3,2,0,1:T(8,128)(2,1)} %copy.452), channel_id=1, replica_groups=mesh['batch'=8,'tensor'=32] {'batch'}, dimensions={1}, use_global_device_ids=true | all-gather | bytes 294912 | tf_op jit(solution)/shard_map/all_gather | solution.py:94
  82.1 1.9 collective-permute-start.1
  86.1 2.0 collective-permute-start.2
  88.1 3.2 collective-permute-done.1
  92.1 10.5 %collective-permute-done = f32[4,8,32,64]{3,1,0,2:T(8,128)S(1)} collective-permute-done((f32[4,8,32,64]{3,1,0,2:T(8,128)S(1)}, f32[4,8,32,64]{3,1,0,2:T(8,128)S(1)}, u32[]{:S(2)}, u32[]{:S(2)}) %collective-permute-start) | collective-permute-done | bytes 262176 | tf_op jit(solution)/shard_map/ppermute | solution.py:14
  103.0 4.6 %collective-permute-done.2 = f32[4,8,4,512]{3,1,0,2:T(8,128)S(1)} collective-permute-done((f32[4,8,4,512]{3,1,0,2:T(8,128)S(1)}, f32[4,8,4,512]{3,1,0,2:T(8,128)S(1)}, u32[]{:S(2)}, u32[]{:S(2)}) %collective-permute-start.2) | collective-permute-done | bytes 262176 | tf_op jit(solution)/shard_map/ppermute | solution.py:14
  112.7 1.7 fusion.23
  116.6 1.7 fusion.31
  121.2 1.5 broadcast_in_dim.190
  124.2 1.5 broadcast_in_dim.187
  127.1 2.0 copy.479
  129.1 2.0 copy.480
  133.6 1.9 convolution_bitcast_fusion.1
  137.3 18.9 %all_to_all.10 = f32[4,8,32,130]{3,0,2,1:T(4,128)S(1)} all-to-all(f32[4,8,32,130]{3,0,2,1:T(4,128)S(1)} %copy.481), channel_id=1, replica_groups=mesh['batch'=8,'tensor'=32] {'batch'}, dimensions={1} | all-to-all | bytes 1064960 | tf_op jit(solution)/shard_map/all_to_all | solution.py:186
  163.0 3.0 fusion.13
  166.0 5.0 %fusion = f32[32,4,4096]{2,0,1:T(8,128)} fusion(f32[4,32,4096]{2,1,0:T(8,128)} %fusion.13, bf16[256,4096]{1,0:T(8,128)(2,1)S(1)} %copy-done, bf16[4096,256]{1,0:T(8,128)(2,1)} %param.21, bf16[32,4,1,4096]{3,1,2,0:T(4,128)(2,1)S(1)} %all-to-all-done, f32[256]{0:T(256)S(1)} %copy-done.23), kind=kOutput, calls=%fused_computation.12 | convolution fusion | flops 537722880 | bytes 9438208 | tf_op jit(solution)/shard_map/srf,fd->rsd/dot_general | solution.py:197
  171.0 4.3 %copy.488 = f32[32,4,4096]{2,1,0:T(4,128)} copy(f32[32,4,4096]{2,0,1:T(8,128)} %fusion) | data formatting | bytes 4194304 | tf_op jit(solution)/shard_map/add | solution.py:195
  176.5 153.5 %all-reduce.3.cloned.1.call-done = f32[32,4,4096]{2,1,0:T(4,128)} async-done(((f32[32,4,4096]{2,1,0:T(4,128)}), f32[32,4,4096]{2,1,0:T(4,128)}) %all-reduce.3.cloned.1.call-update) | async-done | bytes 2097168
  (175 shorter events, 66.7 us)
Async XLA Ops:
  6.5 159.5 %copy-start = (bf16[256,4096]{1,0:T(8,128)(2,1)S(1)}, bf16[256,4096]{1,0:T(8,128)(2,1)}, u32[]{:S(2)}) copy-start(bf16[256,4096]{1,0:T(8,128)(2,1)} %param.23) | copy-start | bytes 6291460
  6.5 16.0 %copy-start.18 = (s32[4,8,32]{2,1,0:T(8,128)S(1)}, s32[4,8,32]{2,1,0:T(8,128)}, u32[]{:S(2)}) copy-start(s32[4,8,32]{2,1,0:T(8,128)} %param.29) | copy-start | bytes 12292
  10.9 41.1 %all-to-all-start = ((bf16[32,4,1,4096]{3,1,2,0:T(4,128)(2,1)}), bf16[32,4,1,4096]{3,1,2,0:T(4,128)(2,1)S(1)}, u32[]{:S(2)}, u32[]{:S(2)}) async-start(bf16[32,4,1,4096]{3,1,2,0:T(4,128)(2,1)} %stack.55), calls=%async_computation | async-start | bytes 2097152 | tf_op jit(solution)/shard_map/all_to_all | solution.py:77
  22.4 307.6 %all-reduce.3.cloned.1.call-start = ((), (), s32[]{:S(2)}) async-start(), calls=%async_computation.2 | async-start | bytes 4194304
  38.8 4.9 %copy-start.22 = (s32[32,4]{0,1:T(4,128)S(1)}, s32[32,4]{0,1:T(4,128)}, u32[]{:S(2)}) copy-start(s32[32,4]{0,1:T(4,128)} %param.27) | copy-start | bytes 1540
  38.9 5.2 %copy-start.24 = (s32[32]{0:T(128)S(1)}, s32[32]{0:T(128)}, u32[]{:S(2)}) copy-start(s32[32]{0:T(128)} %param.28) | copy-start | bytes 388
  43.7 58.9 %copy-start.13 = (pred[4,8,32]{1,0,2:T(4,128)(4,1)}, pred[4,8,32]{1,0,2:T(4,128)(4,1)S(1)}, u32[]{:S(2)}) copy-start(pred[4,8,32]{1,0,2:T(4,128)(4,1)S(1)} %copy.444) | copy-start | bytes 3076
  80.8 5.0 %copy-start.9 = (bf16[4,4,1,128,128]{4,3,2,1,0:T(8,128)(2,1)S(1)}, bf16[4,4,1,128,128]{4,3,2,1,0:T(8,128)(2,1)}, u32[]{:S(2)}) copy-start(bf16[4,4,1,128,128]{4,3,2,1,0:T(8,128)(2,1)} %get-tuple-element.14) | copy-start | bytes 1572868
  82.1 9.3 %copy-start.4 = (f32[4,8,32,4]{1,3,0,2:T(4,128)}, f32[4,8,32,4]{1,3,0,2:T(4,128)S(1)}, u32[]{:S(2)}) copy-start(f32[4,8,32,4]{1,3,0,2:T(4,128)S(1)} %convolution_bitcast_fusion.4) | copy-start | bytes 49156
  82.1 26.3 %copy-start.15 = (pred[4,512]{1,0:T(4,128)(4,1)S(1)}, pred[4,512]{1,0:T(4,128)(4,1)}, u32[]{:S(2)}) copy-start(pred[4,512]{1,0:T(4,128)(4,1)} %iota_compare_fusion) | copy-start | bytes 6148
  82.1 26.4 %copy-start.20 = (pred[32]{0:T(512)(128)(4,1)S(1)}, pred[32]{0:T(512)(128)(4,1)}, u32[]{:S(2)}) copy-start(pred[32]{0:T(512)(128)(4,1)} %broadcast_in_dim.174) | copy-start | bytes 100
  82.1 9.3 %collective-permute-start.1 = (f32[4,8,32,4]{1,3,0,2:T(4,128)S(1)}, f32[4,8,32,4]{1,3,0,2:T(4,128)S(1)}, u32[]{:S(2)}, u32[]{:S(2)}) collective-permute-start(f32[4,8,32,4]{1,3,0,2:T(4,128)S(1)} %convolution_bitcast_fusion.4), channel_id=1, source_target_pairs={{0,1},{1,0},{2,3},{3,2},{4,5},{5,4},{6,7},{7,6},{8,9},{9,8},{10,11... | collective-permute-start | bytes 49160 | tf_op jit(solution)/shard_map/ppermute | solution.py:14
  85.4 17.2 %copy-start.2 = (f32[4,8,32,64]{3,1,0,2:T(8,128)}, f32[4,8,32,64]{3,1,0,2:T(8,128)S(1)}, u32[]{:S(2)}) copy-start(f32[4,8,32,64]{3,1,0,2:T(8,128)S(1)} %convolution_bitcast_fusion.2) | copy-start | bytes 786436
  85.4 17.2 %collective-permute-start = (f32[4,8,32,64]{3,1,0,2:T(8,128)S(1)}, f32[4,8,32,64]{3,1,0,2:T(8,128)S(1)}, u32[]{:S(2)}, u32[]{:S(2)}) collective-permute-start(f32[4,8,32,64]{3,1,0,2:T(8,128)S(1)} %convolution_bitcast_fusion.2), channel_id=1, source_target_pairs={{0,1},{1,0},{2,3},{3,2},{4,5},{5,4},{6,7},{7,6},{8,9},{9,8},{10,11... | collective-permute-start | bytes 786440 | tf_op jit(solution)/shard_map/ppermute | solution.py:14
  86.1 21.6 %collective-permute-start.2 = (f32[4,8,4,512]{3,1,0,2:T(8,128)S(1)}, f32[4,8,4,512]{3,1,0,2:T(8,128)S(1)}, u32[]{:S(2)}, u32[]{:S(2)}) collective-permute-start(f32[4,8,4,512]{3,1,0,2:T(8,128)S(1)} %convolution_bitcast_fusion.3), channel_id=1, source_target_pairs={{0,1},{1,0},{2,3},{3,2},{4,5},{5,4},{6,7},{7,6},{8,9},{9,8},{10,11... | collective-permute-start | bytes 786440 | tf_op jit(solution)/shard_map/ppermute | solution.py:14
  102.6 5.9 %copy-start.8 = (f32[4,8,32,64]{3,1,0,2:T(8,128)}, f32[4,8,32,64]{3,1,0,2:T(8,128)S(1)}, u32[]{:S(2)}) copy-start(f32[4,8,32,64]{3,1,0,2:T(8,128)S(1)} %collective-permute-done) | copy-start | bytes 786436
  103.0 22.7 %copy-start.21 = (pred[32]{0:T(512)(128)(4,1)S(1)}, pred[32]{0:T(512)(128)(4,1)}, u32[]{:S(2)}) copy-start(pred[32]{0:T(512)(128)(4,1)} %broadcast_in_dim.174) | copy-start | bytes 100
  111.3 19.7 %copy-start.16 = (pred[4,512]{1,0:T(4,128)(4,1)S(1)}, pred[4,512]{1,0:T(4,128)(4,1)}, u32[]{:S(2)}) copy-start(pred[4,512]{1,0:T(4,128)(4,1)} %iota_compare_fusion) | copy-start | bytes 6148
  133.5 1.9 copy-start.5
  133.5 1.9 copy-start.11
  133.5 1.9 copy-start.14
  161.3 4.7 %copy-start.23 = (f32[256]{0:T(256)S(1)}, f32[256]{0:T(256)}, u32[]{:S(2)}) copy-start(f32[256]{0:T(256)} %param.22) | copy-start | bytes 3076
  175.3 154.8 %copy-start.12 = (bf16[4,1,1,4096]{3,0,2,1:T(4,128)(2,1)S(1)}, bf16[4,1,1,4096]{3,0,2,1:T(4,128)(2,1)}, u32[]{:S(2)}) copy-start(bf16[4,1,1,4096]{3,0,2,1:T(4,128)(2,1)} %param.16) | copy-start | bytes 98308
  175.3 154.8 %copy-start.19 = (f32[4096]{0:T(1024)S(1)}, f32[4096]{0:T(1024)}, u32[]{:S(2)}) copy-start(f32[4096]{0:T(1024)} %param.24) | copy-start | bytes 49156
  (7 other events, 7.2 us)
Sparse Core Ops, SparseCore 0:
  175.4 154.6 all-reduce.2
